TPU v7x, 32 devices: a whole 2x2x4 slice. The times are simulated.
32 devices in a mesh: rep: 8 (over z, x), shard: 4 (over y, core).
Axes of the slice: x: 2, y: 2, z: 4, core: 2. Of those that a mesh axis runs over, the one named last changes fastest.
Arguments:
- tokens: bfloat16 [32, 384, 1024], P(('rep', 'shard')), may hold values from -6 to 6
- cont_segment: int32 [32, 2, 64], P(('rep', 'shard')), may hold values from 0 to 1, as said below
- cotangent: bfloat16 [32, 384, 1024], P(('rep', 'shard')), may hold values from -6 to 6
- ln1_gain: bfloat16 [1024], P('shard'), may hold values from 0.099609375 to 1.8984375
- ln1_bias: bfloat16 [1024], P('shard'), may hold values from -3 to 3
- w_qkv: bfloat16 [1024, 3072], P(None, 'shard'), may hold values from -0.1875 to 0.1875
- q_bias: bfloat16 [1024], P('shard'), may hold values from -3 to 3
- v_bias: bfloat16 [1024], P('shard'), may hold values from -3 to 3
- w_out: bfloat16 [1024, 1024], P('shard'), may hold values from -0.75 to 0.75
- b_out: bfloat16 [1024], P('shard'), may hold values from -3 to 3
- ln2_gain: bfloat16 [1024], P('shard'), may hold values from 0.099609375 to 1.8984375
- ln2_bias: bfloat16 [1024], P('shard'), may hold values from -3 to 3
- w_up: bfloat16 [1024, 4096], P(None, 'shard'), may hold values from -0.1875 to 0.1875
- b_up: bfloat16 [4096], P('shard'), may hold values from -3 to 3
- w_down: bfloat16 [4096, 1024], P('shard'), may hold values from -0.125 to 0.125
- b_down: bfloat16 [1024], P('shard'), may hold values from -3 to 3
Outputs:
- layer_out: bfloat16 [32, 384, 1024], P(('rep', 'shard'))
- grad_tokens: bfloat16 [32, 384, 1024], P(('rep', 'shard'))
- grad_ln1_gain: float32 [1024], P('shard')
- grad_ln1_bias: float32 [1024], P('shard')
- grad_w_qkv: float32 [1024, 3072], P(None, 'shard')
- grad_q_bias: float32 [1024], P('shard')
- grad_v_bias: float32 [1024], P('shard')
- grad_w_out: float32 [1024, 1024], P('shard')
- grad_b_out: float32 [1024], P('shard')
- grad_ln2_gain: float32 [1024], P('shard')
- grad_ln2_bias: float32 [1024], P('shard')
- grad_w_up: float32 [1024, 4096], P(None, 'shard')
- grad_b_up: float32 [4096], P('shard')
- grad_w_down: float32 [4096, 1024], P('shard')
- grad_b_down: float32 [1024], P('shard')
Inputs may be any that keep to these rules, and one draw needn't show every extreme that they name: `cont_segment`: each micro-batch holds 2 continuations, numbers never falling, each of 16 to 48 rows; in the first micro-batch of every prompt one continuation has exactly 48 rows.
All inputs are finite; a program needn't handle non-finite values.
Results may differ from a plain program's by a relative error of at most 0.015.
Values may be sent and summed in bfloat16 or wider, within the bound.
No kernel may reach another device: no remote copies, remote signals or barrier semaphores. Data moves between devices by JAX's collectives and lax.ppermute only.
A program may use at most 256 MiB of HBM per device.

v0:
```python
from functools import partial
import jax
import jax.numpy as jnp
from jax import lax
from jax.sharding import PartitionSpec as P

HEADS = 16
HDIM = 64
PROMPT = 256


def normalize(values, gain, shift):
    center = values - jnp.mean(values, -1, keepdims=True)
    spread = jnp.mean(center * center, -1, keepdims=True)
    return center * lax.rsqrt(spread + 1e-05) * gain + shift


def layout(segments):
    micros, row_count = segments.shape
    same_seg = segments[:, :, None] == segments[:, None, :]
    earlier = jnp.arange(row_count)[None, :] < jnp.arange(row_count)[:, None]
    offsets = jnp.sum(jnp.where(same_seg & earlier[None], 1, 0), -1).astype(jnp.int32)
    cont_pos = PROMPT + offsets
    owners = jnp.arange(micros, dtype=jnp.int32)[:, None] * row_count + segments
    positions = jnp.concatenate([jnp.arange(PROMPT, dtype=jnp.int32), cont_pos.reshape(-1)])
    groups = jnp.concatenate([jnp.full((PROMPT,), -1, jnp.int32), owners.reshape(-1)])
    places = jnp.arange(positions.shape[0], dtype=jnp.int32)
    allowed = (places[None, :] <= places[:, None]) & (
        (places[None, :] < PROMPT) | (groups[None, :] == groups[:, None])
    )
    distance = (positions[:, None] - positions[None, :]).astype(jnp.float32)
    return (distance, allowed)


def head_slice(matrix, block):
    block_width = 4 * HDIM
    part = lax.dynamic_slice_in_dim(matrix, block * block_width, block_width, 1)
    return part.reshape(matrix.shape[0], 4, HDIM)


def block_scores(q_part, k_part, block, distance, allowed):
    heads = (block * 4 + jnp.arange(4, dtype=jnp.int32)).astype(jnp.float32)
    slopes = jnp.exp2(-8.0 * (heads + 1.0) / HEADS)
    scores = jnp.einsum(
        "qhd,khd->hqk", q_part, k_part, preferred_element_type=jnp.float32
    ) * HDIM ** (-0.5)
    scores = scores - slopes[:, None, None] * distance[None]
    return jnp.where(allowed[None], scores, -jnp.inf)


def side_by_side(blocks):
    return jnp.transpose(blocks, (1, 0, 2)).reshape(
        blocks.shape[1], blocks.shape[0] * blocks.shape[2]
    )


def attend_forward(queries, key_rows, values, distance, allowed):
    length = queries.shape[0]

    def head_block(block):
        q_part = head_slice(queries, block)
        k_part = head_slice(key_rows, block)
        v_part = head_slice(values, block)
        scores = block_scores(q_part, k_part, block, distance, allowed)
        peak = jnp.max(scores, -1, keepdims=True)
        exps_rel = jnp.exp(scores - peak)
        row_totals = jnp.sum(exps_rel, -1, keepdims=True)
        attn_probs = (exps_rel / row_totals).astype(jnp.bfloat16)
        mixed = jnp.einsum("hqk,khd->qhd", attn_probs, v_part, preferred_element_type=jnp.float32)
        return (mixed.reshape(length, 4 * HDIM), (peak + jnp.log(row_totals))[:, :, 0])

    mixed, log_norms = lax.map(head_block, jnp.arange(HEADS // 4, dtype=jnp.int32))
    return (side_by_side(mixed).astype(jnp.bfloat16), log_norms)


def attend_backward(queries, key_rows, values, grad_mixed, log_norms, distance, allowed):
    length = queries.shape[0]
    scale = HDIM ** (-0.5)

    def head_block(block):
        q_part = head_slice(queries, block)
        k_part = head_slice(key_rows, block)
        v_part = head_slice(values, block)
        g_part = head_slice(grad_mixed, block)
        scores = block_scores(q_part, k_part, block, distance, allowed)
        attn_probs = jnp.exp(scores - log_norms[block][:, :, None])
        grad_probs = jnp.einsum("qhd,khd->hqk", g_part, v_part, preferred_element_type=jnp.float32)
        inner = jnp.sum(attn_probs * grad_probs, -1, keepdims=True)
        grad_scores = (attn_probs * (grad_probs - inner)).astype(jnp.bfloat16)
        grad_q = (
            jnp.einsum("hqk,khd->qhd", grad_scores, k_part, preferred_element_type=jnp.float32)
            * scale
        )
        grad_k = (
            jnp.einsum("hqk,qhd->khd", grad_scores, q_part, preferred_element_type=jnp.float32)
            * scale
        )
        grad_v = jnp.einsum(
            "hqk,qhd->khd",
            attn_probs.astype(jnp.bfloat16),
            g_part,
            preferred_element_type=jnp.float32,
        )
        block_width = 4 * HDIM
        return (
            grad_q.reshape(length, block_width),
            grad_k.reshape(length, block_width),
            grad_v.reshape(length, block_width),
        )

    grad_q, grad_k, grad_v = lax.map(head_block, jnp.arange(HEADS // 4, dtype=jnp.int32))
    return (
        side_by_side(grad_q).astype(jnp.bfloat16),
        side_by_side(grad_k).astype(jnp.bfloat16),
        side_by_side(grad_v).astype(jnp.bfloat16),
    )


SMALL = (
    "ln1_gain",
    "ln1_bias",
    "q_bias",
    "v_bias",
    "b_out",
    "ln2_gain",
    "ln2_bias",
    "b_up",
    "b_down",
)


def gather_small(pieces):
    packed = jnp.concatenate(pieces)
    shards = lax.all_gather(packed, "shard", axis=0, tiled=False)
    fulls, offset = ([], 0)
    for piece in pieces:
        width = piece.shape[0]
        fulls.append(shards[:, offset : offset + width].reshape(-1))
        offset += width
    return fulls


def body(
    tokens,
    cont_segment,
    cotangent,
    ln1_gain,
    ln1_bias,
    w_qkv,
    q_bias,
    v_bias,
    w_out,
    b_out,
    ln2_gain,
    ln2_bias,
    w_up,
    b_up,
    w_down,
    b_down,
):
    shard_count = lax.psum(1, "shard")
    full_g1, full_s1, full_qb, full_vb, full_bo, full_g2, full_s2, full_bu, full_bd = gather_small(
        [ln1_gain, ln1_bias, q_bias, v_bias, b_out, ln2_gain, ln2_bias, b_up, b_down]
    )
    full_qkv = lax.all_gather(w_qkv, "shard", axis=1, tiled=True)
    full_out = lax.all_gather(w_out, "shard", axis=0, tiled=True)
    full_up = lax.all_gather(w_up, "shard", axis=1, tiled=True)
    full_down = lax.all_gather(w_down, "shard", axis=0, tiled=True)
    inputs = tokens[0].astype(jnp.float32)
    length, model_width = inputs.shape
    distance, allowed = layout(cont_segment[0])
    normed = normalize(inputs, full_g1.astype(jnp.float32), full_s1.astype(jnp.float32)).astype(
        jnp.bfloat16
    )
    projected = jnp.dot(normed, full_qkv, preferred_element_type=jnp.float32)
    queries = (projected[:, :model_width] + full_qb.astype(jnp.float32)).astype(jnp.bfloat16)
    key_rows = projected[:, model_width : 2 * model_width].astype(jnp.bfloat16)
    values = (projected[:, 2 * model_width :] + full_vb.astype(jnp.float32)).astype(jnp.bfloat16)
    mixed, log_norms = attend_forward(queries, key_rows, values, distance, allowed)
    branch = jnp.dot(mixed, full_out, preferred_element_type=jnp.float32) + full_bo.astype(
        jnp.float32
    )
    middle = inputs + branch
    normed_two = normalize(middle, full_g2.astype(jnp.float32), full_s2.astype(jnp.float32)).astype(
        jnp.bfloat16
    )
    pre_act = jnp.dot(normed_two, full_up, preferred_element_type=jnp.float32) + full_bu.astype(
        jnp.float32
    )
    activated = jax.nn.gelu(pre_act, approximate=True).astype(jnp.bfloat16)
    outputs = middle + (
        jnp.dot(activated, full_down, preferred_element_type=jnp.float32)
        + full_bd.astype(jnp.float32)
    )
    back_g1, back_qkv, back_out, back_g2, back_up, back_down = (
        full_g1,
        full_qkv,
        full_out,
        full_g2,
        full_up,
        full_down,
    )
    cot_low = cotangent[0]
    cot_full = cot_low.astype(jnp.float32)
    zero_shift = jnp.zeros((model_width,), jnp.float32)
    grad_bd = jnp.sum(cot_full, 0)
    grad_act = jnp.einsum("to,fo->tf", cot_low, back_down, preferred_element_type=jnp.float32)
    gelu_value, gelu_pull = jax.vjp(partial(jax.nn.gelu, approximate=True), pre_act)
    grad_pre = gelu_pull(grad_act)[0].astype(jnp.bfloat16)
    grad_bu = jnp.sum(grad_pre.astype(jnp.float32), 0)
    grad_normed_two = jnp.einsum("tf,if->ti", grad_pre, back_up, preferred_element_type=jnp.float32)
    norm_value_two, norm_pull_two = jax.vjp(
        normalize, middle, back_g2.astype(jnp.float32), zero_shift
    )
    grad_mid_part, grad_g2, grad_s2 = norm_pull_two(grad_normed_two)
    grad_middle = cot_full + grad_mid_part
    grad_branch = grad_middle.astype(jnp.bfloat16)
    grad_bo = jnp.sum(grad_branch.astype(jnp.float32), 0)
    grad_mixed = jnp.einsum(
        "to,io->ti", grad_branch, back_out, preferred_element_type=jnp.float32
    ).astype(jnp.bfloat16)
    grad_q, grad_k, grad_v = attend_backward(
        queries, key_rows, values, grad_mixed, log_norms, distance, allowed
    )
    grad_proj = jnp.concatenate([grad_q, grad_k, grad_v], 1)
    grad_qb = jnp.sum(grad_q.astype(jnp.float32), 0)
    grad_vb = jnp.sum(grad_v.astype(jnp.float32), 0)
    grad_normed = jnp.einsum("tc,ic->ti", grad_proj, back_qkv, preferred_element_type=jnp.float32)
    norm_value_one, norm_pull_one = jax.vjp(
        normalize, inputs, back_g1.astype(jnp.float32), zero_shift
    )
    grad_in_part, grad_g1, grad_s1 = norm_pull_one(grad_normed)
    grad_inputs = grad_middle + grad_in_part
    grad_down = jnp.einsum("tf,to->fo", activated, cot_low, preferred_element_type=jnp.float32)
    grad_up = jnp.einsum("ti,tf->if", normed_two, grad_pre, preferred_element_type=jnp.float32)
    grad_out = jnp.einsum("ti,to->io", mixed, grad_branch, preferred_element_type=jnp.float32)
    grad_qkv = jnp.einsum("ti,tc->ic", normed, grad_proj, preferred_element_type=jnp.float32)
    smalls = [grad_g1, grad_s1, grad_qb, grad_vb, grad_bo, grad_g2, grad_s2, grad_bu, grad_bd]
    small_rows = jnp.concatenate([g.reshape(shard_count, -1) for g in smalls], 1)
    small_rows = small_rows.reshape(shard_count, -1, model_width)
    small_rows = jnp.pad(small_rows, ((0, 0), (0, 16 - small_rows.shape[1]), (0, 0)))
    down_rows = grad_down.reshape(shard_count, -1, model_width)
    down_width = down_rows.shape[1] * model_width
    joined = jnp.concatenate([down_rows, small_rows], 1).reshape(-1, model_width)
    joined_own = lax.psum_scatter(
        joined.astype(jnp.bfloat16), "shard", scatter_dimension=0, tiled=True
    ).reshape(-1)
    qkv_own = lax.psum_scatter(
        grad_qkv.astype(jnp.bfloat16), "shard", scatter_dimension=1, tiled=True
    )
    out_own = lax.psum_scatter(
        grad_out.astype(jnp.bfloat16), "shard", scatter_dimension=0, tiled=True
    )
    up_own = lax.psum_scatter(
        grad_up.astype(jnp.bfloat16), "shard", scatter_dimension=1, tiled=True
    )
    owned = [qkv_own, out_own, up_own, joined_own]
    flat = jnp.concatenate([o.reshape(-1).astype(jnp.float32) for o in owned])
    total = lax.psum(flat, "rep")
    pieces, offset = ([], 0)
    for o in owned:
        pieces.append(total[offset : offset + o.size].reshape(o.shape))
        offset += o.size
    qkv_fin, out_fin, up_fin, joined_fin = pieces
    down_fin = joined_fin[:down_width].reshape(grad_down.shape[0] // shard_count, -1)
    small_fin, offset = ([], down_width)
    for g in smalls:
        width = g.shape[0] // shard_count
        small_fin.append(joined_fin[offset : offset + width])
        offset += width
    g1_fin, s1_fin, qb_fin, vb_fin, bo_fin, g2_fin, s2_fin, bu_fin, bd_fin = small_fin
    return (
        outputs.astype(jnp.bfloat16)[None],
        grad_inputs.astype(jnp.bfloat16)[None],
        g1_fin,
        s1_fin,
        qkv_fin,
        qb_fin,
        vb_fin,
        out_fin,
        bo_fin,
        g2_fin,
        s2_fin,
        up_fin,
        bu_fin,
        down_fin,
        bd_fin,
    )


def solution(mesh):
    return jax.shard_map(
        body,
        mesh=mesh,
        in_specs=(
            P(("rep", "shard"), None, None),
            P(("rep", "shard"), None, None),
            P(("rep", "shard"), None, None),
            P("shard"),
            P("shard"),
            P(None, "shard"),
            P("shard"),
            P("shard"),
            P("shard", None),
            P("shard"),
            P("shard"),
            P("shard"),
            P(None, "shard"),
            P("shard"),
            P("shard", None),
            P("shard"),
        ),
        out_specs=(
            P(("rep", "shard"), None, None),
            P(("rep", "shard"), None, None),
            P("shard"),
            P("shard"),
            P(None, "shard"),
            P("shard"),
            P("shard"),
            P("shard", None),
            P("shard"),
            P("shard"),
            P("shard"),
            P(None, "shard"),
            P("shard"),
            P("shard", None),
            P("shard"),
        ),
        check_vma=False,
    )
```

profile of v0, /device:TPU:0, one launch (start us, length us, event | category | flops | bytes accessed | tf_op | source)
XLA Modules:
  0.0 967.9 jit_solution(11583978581339955561)
XLA Ops:
  12.2 6.3 all-gather
  20.3 38.4 %all-gather.6.cloned.1.call-done = bf16[1024,3072]{1,0:T(8,128)(2,1)} async-done(((bf16[1024,768]{1,0:T(8,128)(2,1)}), bf16[1024,3072]{1,0:T(8,128)(2,1)}) %all-gather.6.cloned.1.call-update) | async-done | bytes 6291472 | tf_op jit(solution)/shard_map/all_gather | solution.py:165
  58.7 5.1 fusion.69
  68.4 19.0 %while.32 = (s32[]{:T(128)}, bf16[4,384,256]{1,2,0:T(8,128)(2,1)}, f32[4,4,384]{2,1,0:T(4,128)S(1)}, s32[4]{0:T(128)S(1)}, bf16[384,1024]{0,1:T(8,128)(2,1)S(1)}...) while((s32[]{:T(128)}, bf16[4,384,256]{1,2,0:T(8,128)(2,1)}, ...), condition=%wide.region_6.7_spmd.clone, body=%wide.region_3.6_spmd.clone.sunk | while | flops 157776416 | bytes 10964623 | solution.py:72
  88.6 3.0 fusion.79
  91.9 50.8 %all-gather.10.cloned.1.call-done = bf16[1024,4096]{1,0:T(8,128)(2,1)} async-done(((bf16[1024,1024]{1,0:T(8,128)(2,1)}), bf16[1024,4096]{1,0:T(8,128)(2,1)}) %all-gather.10.cloned.1.call-update) | async-done | bytes 8388624 | tf_op jit(solution)/shard_map/all_gather | solution.py:167
  142.7 11.3 %fusion.30 = (bf16[4096,384]{0,1:T(8,128)(2,1)}, f32[384,4096]{1,0:T(8,128)}) fusion(f32[4096]{0:T(1024)S(1)} %bitcast.254, bf16[1024,4096]{1,0:T(8,128)(2,1)} %all-gather.10.cloned.1.call-done, f32[384,1024]{1,0:T(8,128)S(1)} %get-tuple-element.523, f32[1024]{0:T(1024)S(1)} %bitcast.261, f32[1024]{0:T(1024)S(1)} %bitcast.255, f32[384]{0:T(512)S(1)} %fusion.61, ...), kind=kOutput, calls=%fused_computation.60 | convolution fusion | flops 3238920192 | bytes 19426304 | tf_op jit(solution)/shard_map/dot_general | solution.py:187
  154.0 48.4 %all-gather.12.cloned.1.call-done = bf16[4096,1024]{1,0:T(8,128)(2,1)} async-done(((bf16[1024,1024]{1,0:T(8,128)(2,1)}), bf16[4096,1024]{1,0:T(8,128)(2,1)}) %all-gather.12.cloned.1.call-update) | async-done | bytes 8388624 | tf_op jit(solution)/shard_map/all_gather | solution.py:168
  202.4 10.6 %fusion.80 = (bf16[4096]{0:T(1024)(128)(2,1)S(1)}, bf16[384,4096]{1,0:T(8,128)(2,1)S(1)}) fusion(f32[384,4096]{1,0:T(8,128)} %get-tuple-element.529, bf16[4096,1024]{1,0:T(8,128)(2,1)} %all-gather.12.cloned.1.call-done, bf16[1,384,1024]{2,1,0:T(8,128)(2,1)S(1)} %copy-done.10), kind=kOutput, calls=%fused_computation.158 | convolution fusion | flops 3254251520 | bytes 18620416 | tf_op jit(solution)/shard_map/to,fo->tf/dot_general | solution.py:207
  213.0 3.8 multiply_reduce_fusion.1
  219.2 2.6 convolution_convert_fusion.3
  221.8 2.6 convolution_convert_fusion.4
  227.3 45.8 %while.33 = (s32[]{:T(128)}, bf16[4,384,256]{1,2,0:T(8,128)(2,1)}, bf16[4,384,256]{1,2,0:T(8,128)(2,1)}, bf16[4,384,256]{1,2,0:T(8,128)(2,1)}, s32[4]{0:T(128)S(...) while((s32[]{:T(128)}, bf16[4,384,256]{1,2,0:T(8,128)(2,1)}, ...), condition=%wide.region_13.14_spmd.clone, body=%wide.region_11.13_spmd.clone.sunk | while | flops 385251872 | bytes 36898628 | solution.py:111
  273.1 8.2 convolution_convert_fusion.2
  282.7 9.6 convolution_convert_fusion
  293.8 6.5 fusion.72
  305.3 4.6 copy.86
  309.9 6.6 convolution_convert_fusion.1
  316.6 3.7 fusion.15
  322.3 17.0 %reduce-scatter.5.cloned.1.call-done = bf16[1024,768]{1,0:T(8,128)(2,1)} async-done(((bf16[1024,3072]{1,0:T(8,128)(2,1)}), bf16[1024,768]{1,0:T(8,128)(2,1)}) %reduce-scatter.5.cloned.1.call-update) | async-done | bytes 1572880 | tf_op jit(solution)/shard_map/reduce_scatter | solution.py:248
  339.3 4.0 convert_element_type.308
  343.3 69.8 %reduce-scatter.9.cloned.1.call-done = bf16[1024,1024]{1,0:T(8,128)(2,1)} async-done(((bf16[1024,4096]{1,0:T(8,128)(2,1)}), bf16[1024,1024]{1,0:T(8,128)(2,1)}) %reduce-scatter.9.cloned.1.call-update) | async-done | bytes 2097168 | tf_op jit(solution)/shard_map/reduce_scatter | solution.py:254
  413.2 3.5 copy.98
  416.7 71.3 %reduce-scatter.11.cloned.1.call-done = bf16[1040,1024]{1,0:T(8,128)(2,1)} async-done(((bf16[4160,1024]{1,0:T(8,128)(2,1)}), bf16[1040,1024]{1,0:T(8,128)(2,1)}) %reduce-scatter.11.cloned.1.call-update) | async-done | bytes 2129936 | tf_op jit(solution)/shard_map/reduce_scatter | solution.py:245
  488.1 2.4 copy.99
  490.8 48.4 %maximum_convert_fusion = f32[3162112]{0:T(1024)} fusion(bf16[1064960]{0:T(1024)(128)(2,1)S(1)} %bitcast.226, bf16[1048576]{0:T(1024)(128)(2,1)S(1)} %bitcast.227, bf16[262144]{0:T(1024)(128)(2,1)S(1)} %bitcast.240, bf16[786432]{0:T(1024)(128)(2,1)S(1)} %copy-done.12), kind=kLoop, calls=%fused_computation.45 | loop fusion | flops 25296896 | bytes 18972672 | tf_op jit(solution)/shard_map/concatenate | solution.py:258
  539.9 3.5 fusion.54
  543.4 11.1 %fusion.51 = bf16[1,384,1024]{2,1,0:T(8,128)(2,1)} fusion(f32[384,1024]{1,0:T(8,128)S(1)} %copy-done.3, bf16[4096,1024]{1,0:T(8,128)(2,1)} %all-gather.12.cloned.1.call-done, f32[384,4096]{1,0:T(8,128)} %get-tuple-element.529, f32[1024]{0:T(1024)S(1)} %bitcast.263), kind=kOutput, calls=%fused_computation.101 | convolution fusion | flops 3236560896 | bytes 17043456 | tf_op jit(solution)/shard_map/dot_general | solution.py:192
  554.4 380.6 %all-reduce.4.cloned.1.call-done = f32[3162112]{0:T(1024)} async-done(((f32[3162112]{0:T(1024)}), f32[3162112]{0:T(1024)}) %all-reduce.4.cloned.1.call-update) | async-done | bytes 12648464 | tf_op jit(solution)/shard_map/psum | solution.py:259
  941.2 7.4 fusion.78
  948.6 4.9 slice.140
  953.5 4.9 slice.143
  (312 shorter events, 83.3 us)
Async XLA Ops:
  7.2 51.5 %all-gather.6.cloned.1.call-start = ((), (), s32[]{:S(2)}) async-start(), calls=%async_computation.4 | async-start | bytes 7864320 | tf_op jit(solution)/shard_map/all_gather | solution.py:165
  7.9 2.7 copy-start.23
  7.9 2.9 copy-start.24
  8.0 3.1 copy-start.25
  8.0 3.4 copy-start.26
  8.0 3.6 copy-start.27
  8.0 3.8 copy-start.20
  8.0 4.0 copy-start.28
  8.0 79.4 %all-gather.8.cloned.1.call-start = ((), (), s32[]{:S(2)}) async-start(), calls=%async_computation.5 | async-start | bytes 2621440 | tf_op jit(solution)/shard_map/all_gather | solution.py:166
  8.8 10.5 %copy-start.19 = (s32[1,2,64]{2,1,0:T(2,128)S(1)}, s32[1,2,64]{2,1,0:T(2,128)}, u32[]{:S(2)}) copy-start(s32[1,2,64]{2,1,0:T(2,128)} %param.21) | copy-start | bytes 1540
  8.8 10.9 %copy-start = (bf16[1,384,1024]{2,1,0:T(8,128)(2,1)S(1)}, bf16[1,384,1024]{2,1,0:T(8,128)(2,1)}, u32[]{:S(2)}) copy-start(bf16[1,384,1024]{2,1,0:T(8,128)(2,1)} %param.20) | copy-start | bytes 2359300
  8.8 133.9 %all-gather.10.cloned.1.call-start = ((), (), s32[]{:S(2)}) async-start(), calls=%async_computation.6 | async-start | bytes 10485760 | tf_op jit(solution)/shard_map/all_gather | solution.py:167
  9.5 192.9 %all-gather.12.cloned.1.call-start = ((), (), s32[]{:S(2)}) async-start(), calls=%async_computation.7 | async-start | bytes 10485760 | tf_op jit(solution)/shard_map/all_gather | solution.py:168
  10.1 310.3 %reduce-scatter.7.cloned.1.call-start = ((), (), s32[]{:S(2)}) async-start(), calls=%async_computation.9 | async-start | bytes 2621440 | tf_op jit(solution)/shard_map/reduce_scatter | solution.py:251
  91.6 125.3 %copy-start.2 = (f32[384,1024]{1,0:T(8,128)}, f32[384,1024]{1,0:T(8,128)S(1)}, u32[]{:S(2)}) copy-start(f32[384,1024]{1,0:T(8,128)S(1)} %get-tuple-element.523) | copy-start | bytes 4718596
  142.7 59.7 %copy-start.10 = (bf16[1,384,1024]{2,1,0:T(8,128)(2,1)S(1)}, bf16[1,384,1024]{2,1,0:T(8,128)(2,1)}, u32[]{:S(2)}) copy-start(bf16[1,384,1024]{2,1,0:T(8,128)(2,1)} %param.22) | copy-start | bytes 2359300
  202.4 10.6 %copy-start.29 = (bf16[1024,4096]{1,0:T(8,128)(2,1)S(1)}, bf16[1024,4096]{1,0:T(8,128)(2,1)}, u32[]{:S(2)}) copy-start(bf16[1024,4096]{1,0:T(8,128)(2,1)} %all-gather.10.cloned.1.call-done) | copy-start | bytes 25165828
  213.0 3.8 copy-start.30
  221.7 117.6 %reduce-scatter.5.cloned.1.call-start = ((), (), s32[]{:S(2)}) async-start(), calls=%async_computation.8 | async-start | bytes 7864320 | tf_op jit(solution)/shard_map/reduce_scatter | solution.py:248
  227.5 2.6 copy-start.5
  227.5 2.6 copy-start.16
  239.0 2.5 copy-start.5
  239.0 2.6 copy-start.16
  250.3 2.5 copy-start.5
  250.3 2.6 copy-start.16
  261.7 2.5 copy-start.5
  261.7 2.6 copy-start.16
  281.3 131.9 %reduce-scatter.9.cloned.1.call-start = ((), (), s32[]{:S(2)}) async-start(), calls=%async_computation.10 | async-start | bytes 10485760 | tf_op jit(solution)/shard_map/reduce_scatter | solution.py:254
  292.4 195.7 %reduce-scatter.11.cloned.1.call-start = ((), (), s32[]{:S(2)}) async-start(), calls=%async_computation.11 | async-start | bytes 10649600 | tf_op jit(solution)/shard_map/reduce_scatter | solution.py:245
  320.3 614.7 %all-reduce.4.cloned.1.call-start = ((), (), s32[]{:S(2)}) async-start(), calls=%async_computation.12 | async-start | bytes 25296896 | tf_op jit(solution)/shard_map/psum | solution.py:259
  488.0 2.7 copy-start.12
  488.0 2.8 copy-start.15
  (22 other events, 36.1 us)
Sparse Core Ops, SparseCore 0:
  9.6 49.0 all-gather.5
  60.2 22.5 all-gather.7
  84.4 58.2 all-gather.9
  144.1 58.2 all-gather.11
  221.9 31.1 reduce-scatter.6
  281.4 57.8 reduce-scatter.4
  341.9 71.2 reduce-scatter.8
  415.8 72.2 reduce-scatter.10
  539.4 395.6 all-reduce.3
where the time goes:
time: 973 us; the launch traced here: 968 us
  waiting for transfers between devices  679 us (70%)
  matrix products  98.6 us (10%)
  local copies, waits for them, and re-layouts  81.8 us (8%)
  other arithmetic  67.5 us (7%)
  loops' own time  19.1 us (2%)
  between operations  14.6 us (2%)
    psum x1, waiting for transfers between devices, body(): total = lax.psum(flat, 'rep')  381 us
    reduce_scatter x1, waiting for transfers between devices, body(): lax.psum_scatter(joined.astype(jnp.bfloat16), 'shard', scatter_dimension=...  71.3 us
    reduce_scatter x1, waiting for transfers between devices, body(): lax.psum_scatter(grad_up.astype(jnp.bfloat16), 'shard', scatter_dimension...  69.8 us
    all_gather x1, waiting for transfers between devices, body(): full_up = lax.all_gather(w_up, 'shard', axis=1, tiled=True)  50.8 us
    all_gather x1, waiting for transfers between devices, body(): full_down = lax.all_gather(w_down, 'shard', axis=0, tiled=True)  48.4 us
    concatenate x1, other arithmetic, body(): flat = jnp.concatenate([o.reshape(-1).astype(jnp.float32) for o in owned])  48.4 us
    all_gather x1, waiting for transfers between devices, body(): full_qkv = lax.all_gather(w_qkv, 'shard', axis=1, tiled=True)  38.4 us
  transfers between devices with their start and end apart: 9, of which 7 were waited for; matrix products, arithmetic and copies ran while one was open for 15% of the time, Pallas kernels for 0%

commit v1 on v0

--- a/solution.py
+++ b/solution.py
@@ -256,7 +256,9 @@
     )
     owned = [qkv_own, out_own, up_own, joined_own]
     flat = jnp.concatenate([o.reshape(-1).astype(jnp.float32) for o in owned])
-    total = lax.psum(flat, "rep")
+    total = flat
+    for hop in (1, 2, 4):
+        total = total + lax.ppermute(total, "rep", [(dev, dev ^ hop) for dev in range(8)])
     pieces, offset = ([], 0)
     for o in owned:
         pieces.append(total[offset : offset + o.size].reshape(o.shape))

time: 973 us -> 1730 us (1.78)
  waiting for transfers between devices: 679 us -> 1380 us
  other arithmetic: 67.5 us -> 122 us
    ppermute x0 -> x3, waiting for transfers between devices: none -> 1070 us  [body(): lax.ppermute(total, 'rep', [(dev, dev ^ hop) for dev in range(8)])]
    psum x1 -> x0, waiting for transfers between devices: 381 us -> none  [body(): total = lax.psum(flat, 'rep')]
    add x0 -> x3, other arithmetic: none -> 60.2 us  [body(): total + lax.ppermute(total, 'rep', [(dev, dev ^ hop) for dev in range(8)])]
  transfers between devices with their start and end apart: 9 -> 11, of which waited for: 7 -> 9; matrix products, arithmetic and copies ran while one was open for 15% -> 8% of each run, Pallas kernels for 0% -> 0%
where the time goes in v1:
time: 1730 us; the launch traced here: 1720 us
  waiting for transfers between devices  1380 us (80%)
  other arithmetic  122 us (7%)
  matrix products  97.6 us (6%)
  local copies, waits for them, and re-layouts  81.3 us (5%)
  loops' own time  19 us (1%)
    ppermute x3, waiting for transfers between devices, body(): lax.ppermute(total, 'rep', [(dev, dev ^ hop) for dev in range(8)])  1070 us
    reduce_scatter x1, waiting for transfers between devices, body(): lax.psum_scatter(joined.astype(jnp.bfloat16), 'shard', scatter_dimension=...  72.7 us
    reduce_scatter x1, waiting for transfers between devices, body(): lax.psum_scatter(grad_up.astype(jnp.bfloat16), 'shard', scatter_dimension...  69.8 us
    add x3, other arithmetic, body(): total + lax.ppermute(total, 'rep', [(dev, dev ^ hop) for dev in range(8)])  60.2 us
    all_gather x1, waiting for transfers between devices, body(): full_up = lax.all_gather(w_up, 'shard', axis=1, tiled=True)  50.5 us
    all_gather x1, waiting for transfers between devices, body(): full_down = lax.all_gather(w_down, 'shard', axis=0, tiled=True)  48.5 us
    concatenate x1, other arithmetic, body(): flat = jnp.concatenate([o.reshape(-1).astype(jnp.float32) for o in owned])  46.8 us
    all_gather x1, waiting for transfers between devices, body(): full_qkv = lax.all_gather(w_qkv, 'shard', axis=1, tiled=True)  38.4 us
  transfers between devices with their start and end apart: 11, of which 9 were waited for; matrix products, arithmetic and copies ran while one was open for 8% of the time, Pallas kernels for 0%

profile of v1, /device:TPU:0, one launch (start us, length us, event | category | flops | bytes accessed | tf_op | source)
XLA Modules:
  0.0 1722.4 jit_solution(8200585163310472348)
XLA Ops:
  12.2 6.3 all-gather
  20.3 38.4 %all-gather.6.cloned.1.call-done = bf16[1024,3072]{1,0:T(8,128)(2,1)} async-done(((bf16[1024,768]{1,0:T(8,128)(2,1)}), bf16[1024,3072]{1,0:T(8,128)(2,1)}) %all-gather.6.cloned.1.call-update) | async-done | bytes 6291472 | tf_op jit(solution)/shard_map/all_gather | solution.py:165
  58.7 5.2 fusion.69
  68.5 19.0 %while.32 = (s32[]{:T(128)}, bf16[4,384,256]{1,2,0:T(8,128)(2,1)}, f32[4,4,384]{2,1,0:T(4,128)S(1)}, s32[4]{0:T(128)S(1)}, bf16[384,1024]{0,1:T(8,128)(2,1)S(1)}...) while((s32[]{:T(128)}, bf16[4,384,256]{1,2,0:T(8,128)(2,1)}, ...), condition=%wide.region_6.7_spmd.clone, body=%wide.region_3.6_spmd.clone.sunk | while | flops 157776416 | bytes 10964623 | solution.py:72
  92.2 50.5 %all-gather.10.cloned.1.call-done = bf16[1024,4096]{1,0:T(8,128)(2,1)} async-done(((bf16[1024,1024]{1,0:T(8,128)(2,1)}), bf16[1024,4096]{1,0:T(8,128)(2,1)}) %all-gather.10.cloned.1.call-update) | async-done | bytes 8388624 | tf_op jit(solution)/shard_map/all_gather | solution.py:167
  142.7 11.3 fusion.30
  153.9 48.5 %all-gather.12.cloned.1.call-done = bf16[4096,1024]{1,0:T(8,128)(2,1)} async-done(((bf16[1024,1024]{1,0:T(8,128)(2,1)}), bf16[4096,1024]{1,0:T(8,128)(2,1)}) %all-gather.12.cloned.1.call-update) | async-done | bytes 8388624 | tf_op jit(solution)/shard_map/all_gather | solution.py:168
  202.4 10.9 fusion.81
  213.3 3.8 multiply_reduce_fusion.1
  227.5 49.4 %while.33 = (s32[]{:T(128)}, bf16[4,384,256]{1,2,0:T(8,128)(2,1)}, bf16[4,384,256]{1,2,0:T(8,128)(2,1)}, bf16[4,384,256]{1,2,0:T(8,128)(2,1)}, s32[4]{0:T(128)S(...) while((s32[]{:T(128)}, bf16[4,384,256]{1,2,0:T(8,128)(2,1)}, ...), condition=%wide.region_13.14_spmd.clone, body=%wide.region_11.13_spmd.clone.sunk | while | flops 385251872 | bytes 36898628 | solution.py:111
  276.9 8.2 convolution_convert_fusion.2
  286.6 9.7 convolution_convert_fusion
  298.3 5.9 fusion.73
  306.8 4.7 copy.86
  311.5 6.6 convolution_convert_fusion.1
  318.2 3.8 fusion.15
  323.2 20.1 %reduce-scatter.5.cloned.1.call-done = bf16[1024,768]{1,0:T(8,128)(2,1)} async-done(((bf16[1024,3072]{1,0:T(8,128)(2,1)}), bf16[1024,768]{1,0:T(8,128)(2,1)}) %reduce-scatter.5.cloned.1.call-update) | async-done | bytes 1572880 | tf_op jit(solution)/shard_map/reduce_scatter | solution.py:248
  343.2 4.0 convert_element_type.308
  347.2 69.8 %reduce-scatter.9.cloned.1.call-done = bf16[1024,1024]{1,0:T(8,128)(2,1)} async-done(((bf16[1024,4096]{1,0:T(8,128)(2,1)}), bf16[1024,1024]{1,0:T(8,128)(2,1)}) %reduce-scatter.9.cloned.1.call-update) | async-done | bytes 2097168 | tf_op jit(solution)/shard_map/reduce_scatter | solution.py:254
  419.3 72.7 %reduce-scatter.11.cloned.1.call-done = bf16[1040,1024]{1,0:T(8,128)(2,1)} async-done(((bf16[4160,1024]{1,0:T(8,128)(2,1)}), bf16[1040,1024]{1,0:T(8,128)(2,1)}) %reduce-scatter.11.cloned.1.call-update) | async-done | bytes 2129936 | tf_op jit(solution)/shard_map/reduce_scatter | solution.py:245
  494.3 46.8 %maximum_convert_fusion = f32[3162112]{0:T(1024)S(1)} fusion(bf16[1064960]{0:T(1024)(128)(2,1)S(1)} %bitcast.226, bf16[1048576]{0:T(1024)(128)(2,1)S(1)} %bitcast.228, bf16[262144]{0:T(1024)(128)(2,1)S(1)} %bitcast.234, bf16[786432]{0:T(1024)(128)(2,1)S(1)} %copy-done.3), kind=kLoop, calls=%fused_computation.45 | loop fusion | flops 25296896 | bytes 18972672 | tf_op jit(solution)/shard_map/concatenate | solution.py:258
  542.7 271.9 %collective-permute-done = f32[3162112]{0:T(1024)} collective-permute-done((f32[3162112]{0:T(1024)S(1)}, f32[3162112]{0:T(1024)}, u32[]{:S(2)}, u32[]{:S(2)}) %collective-permute-start) | collective-permute-done | bytes 12648480 | tf_op jit(solution)/shard_map/ppermute | solution.py:261
  814.6 48.6 %fusion.72 = f32[3162112]{0:T(1024)S(1)} fusion(f32[3162112]{0:T(1024)} %collective-permute-done, bf16[1064960]{0:T(1024)(128)(2,1)S(1)} %bitcast.227, bf16[1048576]{0:T(1024)(128)(2,1)S(1)} %bitcast.229, bf16[262144]{0:T(1024)(128)(2,1)S(1)} %bitcast.235, bf16[786432]{0:T(1024)(128)(2,1)S(1)} %copy-done.3), kind=kLoop, calls=%fused_computation.151 | loop fusion | flops 28459008 | bytes 31621120 | tf_op jit(solution)/shard_map/add | solution.py:261
  864.9 271.1 %collective-permute-done.1 = f32[3162112]{0:T(1024)} collective-permute-done((f32[3162112]{0:T(1024)S(1)}, f32[3162112]{0:T(1024)}, u32[]{:S(2)}, u32[]{:S(2)}) %collective-permute-start.1) | collective-permute-done | bytes 12648480 | tf_op jit(solution)/shard_map/ppermute | solution.py:261
  1135.9 5.8 add.282
  1145.9 10.1 fusion.51
  1155.9 529.5 %collective-permute-done.2 = f32[3162112]{0:T(1024)} collective-permute-done((f32[3162112]{0:T(1024)S(1)}, f32[3162112]{0:T(1024)}, u32[]{:S(2)}, u32[]{:S(2)}) %collective-permute-start.2) | collective-permute-done | bytes 12648480 | tf_op jit(solution)/shard_map/ppermute | solution.py:261
  1685.4 5.8 add.283
  1694.1 4.4 fusion.79
  1699.8 4.7 reshape.407
  1705.6 4.9 slice.140
  1710.5 4.9 slice.143
  (327 shorter events, 99.7 us)
Async XLA Ops:
  7.2 51.5 %all-gather.6.cloned.1.call-start = ((), (), s32[]{:S(2)}) async-start(), calls=%async_computation.4 | async-start | bytes 7864320 | tf_op jit(solution)/shard_map/all_gather | solution.py:165
  8.0 3.1 copy-start.30
  8.0 3.4 copy-start.31
  8.0 3.6 copy-start.32
  8.0 3.8 copy-start.25
  8.0 4.0 copy-start.33
  8.0 79.6 %all-gather.8.cloned.1.call-start = ((), (), s32[]{:S(2)}) async-start(), calls=%async_computation.5 | async-start | bytes 2621440 | tf_op jit(solution)/shard_map/all_gather | solution.py:166
  8.8 10.5 copy-start.24
  8.8 10.9 copy-start.1
  8.8 133.9 %all-gather.10.cloned.1.call-start = ((), (), s32[]{:S(2)}) async-start(), calls=%async_computation.6 | async-start | bytes 10485760 | tf_op jit(solution)/shard_map/all_gather | solution.py:167
  9.5 192.9 %all-gather.12.cloned.1.call-start = ((), (), s32[]{:S(2)}) async-start(), calls=%async_computation.7 | async-start | bytes 10485760 | tf_op jit(solution)/shard_map/all_gather | solution.py:168
  10.1 311.9 %reduce-scatter.7.cloned.1.call-start = ((), (), s32[]{:S(2)}) async-start(), calls=%async_computation.9 | async-start | bytes 2621440 | tf_op jit(solution)/shard_map/reduce_scatter | solution.py:251
  91.9 125.3 %copy-start.4 = (f32[384,1024]{1,0:T(8,128)}, f32[384,1024]{1,0:T(8,128)S(1)}, u32[]{:S(2)}) copy-start(f32[384,1024]{1,0:T(8,128)S(1)} %get-tuple-element.523) | copy-start | bytes 4718596
  142.7 59.7 %copy-start.13 = (bf16[1,384,1024]{2,1,0:T(8,128)(2,1)S(1)}, bf16[1,384,1024]{2,1,0:T(8,128)(2,1)}, u32[]{:S(2)}) copy-start(bf16[1,384,1024]{2,1,0:T(8,128)(2,1)} %param.22) | copy-start | bytes 2359300
  202.4 10.9 copy-start.34
  213.3 3.8 copy-start.35
  222.0 121.2 %reduce-scatter.5.cloned.1.call-start = ((), (), s32[]{:S(2)}) async-start(), calls=%async_computation.8 | async-start | bytes 7864320 | tf_op jit(solution)/shard_map/reduce_scatter | solution.py:248
  227.7 3.5 copy-start.21
  240.0 3.5 copy-start.21
  252.3 3.5 copy-start.21
  264.6 3.5 copy-start.21
  285.2 131.9 %reduce-scatter.9.cloned.1.call-start = ((), (), s32[]{:S(2)}) async-start(), calls=%async_computation.10 | async-start | bytes 10485760 | tf_op jit(solution)/shard_map/reduce_scatter | solution.py:254
  296.2 195.8 %reduce-scatter.11.cloned.1.call-start = ((), (), s32[]{:S(2)}) async-start(), calls=%async_computation.11 | async-start | bytes 10649600 | tf_op jit(solution)/shard_map/reduce_scatter | solution.py:245
  541.1 273.5 %collective-permute-start = (f32[3162112]{0:T(1024)S(1)}, f32[3162112]{0:T(1024)}, u32[]{:S(2)}, u32[]{:S(2)}) collective-permute-start(f32[3162112]{0:T(1024)S(1)} %maximum_convert_fusion), channel_id=1, source_target_pairs={{0,4},{4,0},{8,12},{12,8},{16,20},{20,16},{24,28},{28,24},{1,5},{5... | collective-permute-start | bytes 37945352 | tf_op jit(solution)/shard_map/ppermute | solution.py:261
  863.2 281.0 %copy-start.23 = (f32[1,2,4,128]{3,2,1,0:T(4,128)S(1)}, f32[1,2,4,128]{3,2,1,0:T(4,128)}, u32[]{:S(2)}) copy-start(f32[1,2,4,128]{3,2,1,0:T(4,128)} %get-tuple-element.514) | copy-start | bytes 12292
  863.3 281.0 %copy-start.8 = (f32[384,1024]{1,0:T(8,128)S(1)}, f32[384,1024]{1,0:T(8,128)}, u32[]{:S(2)}) copy-start(f32[384,1024]{1,0:T(8,128)} %copy-done.7) | copy-start | bytes 4718596
  863.3 281.0 %copy-start.15 = (bf16[1,384,1024]{2,1,0:T(8,128)(2,1)S(1)}, bf16[1,384,1024]{2,1,0:T(8,128)(2,1)}, u32[]{:S(2)}) copy-start(bf16[1,384,1024]{2,1,0:T(8,128)(2,1)} %param.22) | copy-start | bytes 2359300
  863.3 281.0 %copy-start.17 = (f32[384,1024]{1,0:T(8,128)S(1)}, f32[384,1024]{1,0:T(8,128)}, u32[]{:S(2)}) copy-start(f32[384,1024]{1,0:T(8,128)} %copy-done.16) | copy-start | bytes 4718596
  863.3 272.6 %collective-permute-start.1 = (f32[3162112]{0:T(1024)S(1)}, f32[3162112]{0:T(1024)}, u32[]{:S(2)}, u32[]{:S(2)}) collective-permute-start(f32[3162112]{0:T(1024)S(1)} %fusion.72), channel_id=1, source_target_pairs={{0,8},{4,12},{8,0},{12,4},{16,24},{20,28},{24,16},{28,20},{1,9},{5... | collective-permute-start | bytes 37945352 | tf_op jit(solution)/shard_map/ppermute | solution.py:261
  1141.7 543.7 %collective-permute-start.2 = (f32[3162112]{0:T(1024)S(1)}, f32[3162112]{0:T(1024)}, u32[]{:S(2)}, u32[]{:S(2)}) collective-permute-start(f32[3162112]{0:T(1024)S(1)} %add.282), channel_id=1, source_target_pairs={{0,16},{4,20},{8,24},{12,28},{16,0},{20,4},{24,8},{28,12},{1,17},{... | collective-permute-start | bytes 37945352 | tf_op jit(solution)/shard_map/ppermute | solution.py:261
  1691.2 8.0 copy-start
  1699.8 4.7 slice-start
  (28 other events, 49.0 us)
Sparse Core Ops, SparseCore 0:
  9.6 49.0 all-gather.5
  60.2 22.5 all-gather.7
  84.4 58.2 all-gather.9
  144.1 58.2 all-gather.11
  222.1 31.2 reduce-scatter.6
  285.3 57.9 reduce-scatter.4
  345.8 71.2 reduce-scatter.8
  419.7 72.2 reduce-scatter.10
